TPU v7x, 512 devices: a whole 4x4x16 slice. The times are simulated.
512 devices in a mesh: dp: 64 (over z, x), pair: 8 (over y, core).
Axes of the slice: x: 4, y: 4, z: 16, core: 2. Of those that a mesh axis runs over, the one named last changes fastest.
Arguments:
- embedding: bfloat16 [65536, 1024], P(('dp', 'pair')), may hold values from -32 to 32
- labels: int32 [65536], P(('dp', 'pair')), may hold values from 0 to 127, as said below
- order_ids: int32 [65536], P(('dp', 'pair')), may hold values from 0 to 65535, each once
Outputs:
- best_similarity: float32 [65536], P(('dp', 'pair'))
Inputs may be any that keep to these rules, and one draw needn't show every extreme that they name: `labels`: clusters 2 * g to 2 * g + 1 form owner group g. Among the 128 rows of one device (aligned blocks of the whole array) at most 4 name clusters of any one group, and in every draw some group gets exactly 4 rows from every device.
All inputs are finite; a program needn't handle non-finite values.
Results may differ from a plain program's by a relative error of at most 0.00049.
Values may be sent and summed in bfloat16 or wider, within the bound.
No kernel may reach another device: no remote copies, remote signals or barrier semaphores. Data moves between devices by JAX's collectives and lax.ppermute only.
A program may use at most 64 MiB of HBM per device.

v0:
```python
import jax
import jax.numpy as jnp
from jax import lax
from jax.sharding import PartitionSpec as P

CL_OWN = 2
META = 128
PUBLISH_ROWS = 32


def tile_best(own_rows, own_key, other_rows, other_key, rows_total):
    scores = jnp.dot(own_rows, other_rows.T, preferred_element_type=jnp.float32)
    same_cluster = other_key[None, :] // rows_total == own_key[:, None] // rows_total
    earlier = same_cluster & (other_key[None, :] < own_key[:, None])
    return jnp.max(jnp.where(earlier, scores, -1.0), axis=1)


def slot_keys(rows, width, rows_total):
    meta = rows[:, width : width + 3].astype(jnp.int32)
    return meta[:, 0] * rows_total + meta[:, 1] * 256 + meta[:, 2]


def on_device(embedding, labels, order_ids):
    groups = lax.axis_size("dp")
    pairs = lax.axis_size("pair")
    rows_here, width = embedding.shape
    rows_total = rows_here * groups * pairs
    capacity = 2 * rows_here // groups
    slot_count = groups * capacity
    values = embedding.astype(jnp.float32)
    squares = jnp.sum(values * values, axis=1, keepdims=True)
    shifted = squares + 1e-06
    unit_rows = (values * lax.rsqrt(shifted)).astype(jnp.bfloat16)
    owner_group = labels // CL_OWN
    onehot = (owner_group[:, None] == jnp.arange(groups, dtype=jnp.int32)[None, :]).astype(
        jnp.int32
    )
    before = jnp.cumsum(onehot, axis=0) - onehot
    slot_index = owner_group * capacity + jnp.sum(before * onehot, axis=1)
    meta = jnp.stack([labels + 1, order_ids // 256, order_ids % 256], axis=1).astype(jnp.bfloat16)
    meta = jnp.pad(meta, ((0, 0), (0, META - 3)))
    packed = jnp.concatenate([unit_rows, meta], axis=1)
    send_rows = jnp.zeros((slot_count, width + META), jnp.bfloat16).at[slot_index].set(packed)
    got_rows = lax.all_to_all(
        send_rows.reshape(groups, capacity, -1), "dp", split_axis=0, concat_axis=0, tiled=True
    ).reshape(slot_count, -1)
    piece_rows = lax.all_gather(got_rows, "pair", axis=0, tiled=True)
    got_key = slot_keys(got_rows, width, rows_total)
    piece_key = slot_keys(piece_rows, width, rows_total)
    column = lax.broadcasted_iota(jnp.int32, got_rows.shape, 1)
    query_rows = jnp.where(column < width, got_rows, jnp.zeros_like(got_rows))
    best_seen = jnp.full((slot_count,), -1.0, jnp.float32)
    piece_count = piece_rows.shape[0]
    for offset in range(0, piece_count, 512):
        width_now = min(512, piece_count - offset)
        found = tile_best(
            query_rows,
            got_key,
            piece_rows[offset : offset + width_now],
            piece_key[offset : offset + width_now],
            rows_total,
        )
        best_seen = jnp.maximum(best_seen, found)
    publish = jnp.zeros((PUBLISH_ROWS * 128,), jnp.float32).at[:slot_count].set(best_seen)
    published = lax.all_gather(publish.reshape(PUBLISH_ROWS, 128), "dp", axis=0, tiled=False)
    me = lax.axis_index("dp")
    answered = lax.dynamic_slice_in_dim(
        published.reshape(groups, PUBLISH_ROWS * 128), me * capacity, capacity, axis=1
    )
    return answered.reshape(slot_count)[slot_index]


def solution(mesh):
    in_specs = (P(("dp", "pair"), None), P(("dp", "pair")), P(("dp", "pair")))
    out_specs = P(("dp", "pair"))
    return jax.shard_map(
        on_device, mesh=mesh, in_specs=in_specs, out_specs=out_specs, check_vma=False
    )
```

profile of v0, /device:TPU:8, one launch (start us, length us, event | category | flops | bytes accessed | tf_op | source)
XLA Modules:
  0.0 256.4 jit_solution(14375752796550664068)
XLA Ops:
  6.5 0.7 convert_bitcast_fusion.1
  7.2 0.1 fusion.36
  7.3 0.2 reduce_window_sum.11
  7.5 0.2 select_reduce_fusion
  7.7 0.7 convert_bitcast_fusion
  8.3 0.1 copy.7
  8.5 1.1 fusion.18
  9.6 1.1 fusion.19
  10.6 1.3 scatter_custom_fusion
  12.0 0.1 reshape.149
  12.1 54.0 %all_to_all.5 = bf16[64,4,1152]{2,1,0:T(4,128)(2,1)S(1)} all-to-all(bf16[64,4,1152]{2,1,0:T(4,128)(2,1)S(1)} %reshape.149), channel_id=1, replica_groups=mesh['dp'=64,'pair'=8] {'dp'}, dimensions={0} | all-to-all | bytes 1179648 | tf_op jit(solution)/shard_map/all_to_all | solution.py:44
  66.1 1.0 reshape.150
  67.1 0.0 all-gather.3.cloned.1.call-update
  67.1 0.0 all-gather.5.cloned.1.call-start
  67.2 0.9 slice_convert_fusion.1
  68.1 0.3 fusion.33
  68.4 31.6 %all-gather.3.cloned.1.call-done = bf16[2048,1152]{1,0:T(8,128)(2,1)} async-done(((bf16[256,1152]{1,0:T(8,128)(2,1)}), bf16[2048,1152]{1,0:T(8,128)(2,1)}) %all-gather.3.cloned.1.call-update) | async-done | bytes 4718608 | tf_op jit(solution)/shard_map/all_gather | solution.py:47
  99.9 1.3 slice_convert_fusion
  101.2 0.6 slice_add_fusion
  101.8 0.4 slice_reduce_fusion.3
  102.2 0.2 copy-done.1
  102.4 0.6 fusion.4
  103.1 0.6 fusion.7
  103.7 0.6 fusion.10
  104.4 0.6 fusion.13
  105.0 0.6 pad_bitcast_fusion
  105.6 0.0 all-gather.5.cloned.1.call-update
  105.7 140.1 %all-gather.5.cloned.1.call-done = f32[64,32,128]{2,1,0:T(8,128)} async-done(((f32[1,32,128]{2,1,0:T(8,128)}), f32[64,32,128]{2,1,0:T(8,128)}) %all-gather.5.cloned.1.call-update) | async-done | bytes 1048592 | tf_op jit(solution)/shard_map/all_gather | solution.py:65
  245.8 1.8 copy.10
  247.6 0.1 constant_dynamic-slice_fusion
  247.7 0.1 reshape.152
  247.8 1.8 gather_fusion
  (12 shorter events, 0.1 us)
Async XLA Ops:
  6.5 93.4 %all-gather.3.cloned.1.call-start = ((), (), s32[]{:S(2)}) async-start(), calls=%async_computation.1 | async-start | bytes 5308416 | tf_op jit(solution)/shard_map/all_gather | solution.py:47
  67.1 35.1 %copy-start = (bf16[256,1152]{1,0:T(8,128)(2,1)S(1)}, bf16[256,1152]{1,0:T(8,128)(2,1)}, u32[]{:S(2)}) copy-start(bf16[256,1152]{1,0:T(8,128)(2,1)} %reshape.150) | copy-start | bytes 1769476
  67.1 178.7 %all-gather.5.cloned.1.call-start = ((), (), s32[]{:S(2)}) async-start(), calls=%async_computation.2 | async-start | bytes 1064960 | tf_op jit(solution)/shard_map/all_gather | solution.py:65
  99.9 2.5 copy-start.1
Sparse Core Ops, SparseCore 0:
  67.2 32.6 all-gather.2
  105.8 139.9 all-gather.4
where the time goes:
time: 257 us; the launch traced here: 256 us
  waiting for transfers between devices  172 us (67%)
  blocking collectives  54 us (21%)
  between operations  13.5 us (5%)
  other arithmetic  8.4 us (3%)
  local copies, waits for them, and re-layouts  6.2 us (2%)
    all_gather x1, waiting for transfers between devices, on_device(): lax.all_gather(publish.reshape(PUBLISH_ROWS, 128), 'dp', axis=0, tiled=Fa...  140 us
    all_to_all x1, blocking collectives, on_device(): lax.all_to_all(send_rows.reshape(groups, capacity, -1), 'dp', split_axis=...  54 us
    all_gather x1, waiting for transfers between devices, on_device(): piece_rows = lax.all_gather(got_rows, 'pair', axis=0, tiled=True)  31.6 us
  transfers between devices with their start and end apart: 2, of which 2 were waited for; matrix products, arithmetic and copies ran while one was open for 0% of the time, Pallas kernels for 0%

commit v1 on v0

--- a/solution.py
+++ b/solution.py
@@ -44,7 +44,9 @@
     got_rows = lax.all_to_all(
         send_rows.reshape(groups, capacity, -1), "dp", split_axis=0, concat_axis=0, tiled=True
     ).reshape(slot_count, -1)
-    piece_rows = lax.all_gather(got_rows, "pair", axis=0, tiled=True)
+    piece_rows = jnp.concatenate(
+        lax.all_to_all(jnp.stack([got_rows] * lax.axis_size("pair")), "pair", 0, 0), axis=0
+    )
     got_key = slot_keys(got_rows, width, rows_total)
     piece_key = slot_keys(piece_rows, width, rows_total)
     column = lax.broadcasted_iota(jnp.int32, got_rows.shape, 1)

time: 257 us -> 284 us (1.11)
  local copies, waits for them, and re-layouts: 6.2 us -> 17.5 us
  waiting for transfers between devices: 172 us -> 183 us
  starting transfers between devices: 0.04 us -> 4.92 us
    all_to_all x0 -> x1, waiting for transfers between devices: none -> 53.3 us  [on_device(): lax.all_to_all(jnp.stack([got_rows] * lax.axis_size('pair')), 'pair', 0, 0)]
    all_gather x1 -> x0, waiting for transfers between devices: 31.6 us -> none  [on_device(): piece_rows = lax.all_gather(got_rows, 'pair', axis=0, tiled=True)]
    all_gather x1, waiting for transfers between devices: 140 us -> 130 us  [on_device(): lax.all_gather(publish.reshape(PUBLISH_ROWS, 128), 'dp', axis=0, tiled=Fa...]
    all_to_all x0 -> x1, local copies, waits for them, and re-layouts: none -> 6.78 us  [on_device(): lax.all_to_all(jnp.stack([got_rows] * lax.axis_size('pair')), 'pair', 0, 0)]
    all_to_all x0 -> x1, starting transfers between devices: none -> 4.92 us  [on_device(): lax.all_to_all(jnp.stack([got_rows] * lax.axis_size('pair')), 'pair', 0, 0)]
    another operation x0 -> x3, local copies, waits for them, and re-layouts: none -> 2.85 us  [on_device(): jnp.stack([got_rows] * lax.axis_size('pair'))]
where the time goes in v1:
time: 284 us; the launch traced here: 283 us
  waiting for transfers between devices  183 us (64%)
  blocking collectives  54 us (19%)
  local copies, waits for them, and re-layouts  17.5 us (6%)
  between operations  13.5 us (5%)
  other arithmetic  7.61 us (3%)
  starting transfers between devices  4.92 us (2%)
    all_gather x1, waiting for transfers between devices, on_device(): lax.all_gather(publish.reshape(PUBLISH_ROWS, 128), 'dp', axis=0, tiled=Fa...  130 us
    all_to_all x1, blocking collectives, on_device(): lax.all_to_all(send_rows.reshape(groups, capacity, -1), 'dp', split_axis=...  54 us
    all_to_all x1, waiting for transfers between devices, on_device(): lax.all_to_all(jnp.stack([got_rows] * lax.axis_size('pair')), 'pair', 0, 0)  53.3 us
    all_to_all x1, local copies, waits for them, and re-layouts, on_device(): lax.all_to_all(jnp.stack([got_rows] * lax.axis_size('pair')), 'pair', 0, 0)  6.78 us
  transfers between devices with their start and end apart: 2, of which 2 were waited for; matrix products, arithmetic and copies ran while one was open for 0% of the time, Pallas kernels for 0%

profile of v1, /device:TPU:8, one launch (start us, length us, event | category | flops | bytes accessed | tf_op | source)
XLA Modules:
  0.0 283.1 jit_solution(12305552172805881841)
XLA Ops:
  6.5 1.1 fusion.6
  7.6 0.7 convert_bitcast_fusion.1
  8.3 0.7 convert_bitcast_fusion
  9.0 0.1 copy.18
  9.2 0.2 reduce_window_sum.11
  9.4 0.2 select_reduce_fusion
  9.6 1.1 fusion.7
  10.6 1.3 scatter_custom_fusion
  12.0 0.1 reshape.176
  12.1 54.0 %all_to_all.10 = bf16[64,4,1152]{2,1,0:T(4,128)(2,1)S(1)} all-to-all(bf16[64,4,1152]{2,1,0:T(4,128)(2,1)S(1)} %reshape.176), channel_id=1, replica_groups=mesh['dp'=64,'pair'=8] {'dp'}, dimensions={0} | all-to-all | bytes 1179648 | tf_op jit(solution)/shard_map/all_to_all | solution.py:44
  66.1 0.1 stack_reshape.2
  66.3 0.2 copy.12
  66.5 2.5 stack.23
  69.0 4.9 %all-to-all-start.1 = ((bf16[8,256,1152]{1,2,0:T(8,128)(2,1)}), bf16[8,256,1152]{1,2,0:T(8,128)(2,1)}, u32[]{:S(2)}, u32[]{:S(2)}) async-start(bf16[8,256,1152]{1,2,0:T(8,128)(2,1)} %stack.23), calls=%async_computation.1 | async-start | bytes 9437184 | tf_op jit(solution)/shard_map/all_to_all | solution.py:48
  73.9 0.2 broadcast_select_fusion
  74.2 0.1 select_n.80
  74.3 0.3 fusion.17
  74.6 53.3 %all-to-all-done.1 = bf16[8,256,1152]{1,2,0:T(8,128)(2,1)} async-done(((bf16[8,256,1152]{1,2,0:T(8,128)(2,1)}), bf16[8,256,1152]{1,2,0:T(8,128)(2,1)}, u32[]{:S(2)}, u32[]{:S(2)}) %all-to-all-start.1) | async-done | bytes 4718624 | tf_op jit(solution)/shard_map/all_to_all | solution.py:48
  127.9 6.8 %copy.13 = bf16[8,256,1152]{2,1,0:T(8,128)(2,1)} copy(bf16[8,256,1152]{1,2,0:T(8,128)(2,1)} %all-to-all-done.1) | data formatting | bytes 9437184 | tf_op jit(solution)/shard_map/all_to_all | solution.py:48
  134.7 2.7 fusion.32
  137.4 1.1 slice_convert_fusion
  138.5 0.6 slice_add_fusion
  139.1 0.4 slice_reduce_fusion.3
  139.5 0.6 fusion.1
  140.2 0.6 fusion.2
  140.8 0.6 fusion
  141.5 0.6 fusion.3
  142.1 0.6 pad_bitcast_fusion
  142.8 129.7 %all-gather.2.cloned.1.call-done = f32[64,32,128]{2,1,0:T(8,128)} async-done(((f32[1,32,128]{2,1,0:T(8,128)}), f32[64,32,128]{2,1,0:T(8,128)}) %all-gather.2.cloned.1.call-update) | async-done | bytes 1048592 | tf_op jit(solution)/shard_map/all_gather | solution.py:67
  272.5 1.8 copy.21
  274.4 0.1 reshape.179
  274.5 1.8 gather_fusion
  (13 shorter events, 0.3 us)
Async XLA Ops:
  69.0 58.9 %all-to-all-start.1 = ((bf16[8,256,1152]{1,2,0:T(8,128)(2,1)}), bf16[8,256,1152]{1,2,0:T(8,128)(2,1)}, u32[]{:S(2)}, u32[]{:S(2)}) async-start(bf16[8,256,1152]{1,2,0:T(8,128)(2,1)} %stack.23), calls=%async_computation.1 | async-start | bytes 9437184 | tf_op jit(solution)/shard_map/all_to_all | solution.py:48
  73.9 198.6 %all-gather.2.cloned.1.call-start = ((), (), s32[]{:S(2)}) async-start(), calls=%async_computation.2 | async-start | bytes 1064960 | tf_op jit(solution)/shard_map/all_gather | solution.py:67
Sparse Core Ops, SparseCore 0:
  142.9 129.5 all-gather.1
